TPU v7x, 512 devices: a whole 4x4x16 slice. The times are simulated.
512 devices in a mesh: dom: 16 (over x_hi, y, core), band: 32 (over z, x_lo).
Axes of the slice: x: 4 (x_hi: 2, x_lo: 2; x = x_hi * 2 + x_lo), y: 4, z: 16, core: 2. Of those that a mesh axis runs over, the one named last changes fastest.
Arguments:
- psi: float32 [1024, 192, 2, 384], P('band', 'dom'), may hold values from -6 to 6
- potential: float32 [192, 2, 384], P('dom'), may hold values from -3 to 3
- rotation: bfloat16 [1024, 1024], replicated, may hold values from -0.1875 to 0.1875
Outputs:
- rotated: bfloat16 [1024, 192, 2, 384], P('band', 'dom')
All inputs are finite; a program needn't handle non-finite values.
Results may differ from a plain program's by a relative error of at most 0.005.
Values may be sent and summed in bfloat16 or wider, within the bound.
No kernel may reach another device: no remote copies, remote signals or barrier semaphores. Data moves between devices by JAX's collectives and lax.ppermute only.
A program may use at most 128 MiB of HBM per device.

v0:
```python
import jax
import jax.numpy as jnp
from jax import lax
from jax.sharding import PartitionSpec as P

coeffs = (
    -5369.0 / 1800.0,
    12.0 / 7.0,
    -15.0 / 56.0,
    10.0 / 189.0,
    -1.0 / 112.0,
    2.0 / 1925.0,
    -1.0 / 16632.0,
)
center_shift = 32.5
half_width = 27.5


def extended_2(cells, sides, width):
    for axis, dim in sides:
        count = lax.axis_size(axis)
        head = lax.slice_in_dim(cells, 0, width, axis=dim)
        tail = lax.slice_in_dim(cells, cells.shape[dim] - width, cells.shape[dim], axis=dim)
        cells = jnp.concatenate(
            [
                lax.ppermute(tail, axis, [(i, (i + 1) % count) for i in range(count)]),
                cells,
                lax.ppermute(head, axis, [((i + 1) % count, i) for i in range(count)]),
            ],
            axis=dim,
        )
    return cells


def apply_ham(extended, pot, width):
    middle = extended[:, 6 : 6 + width]
    lap = 3.0 * coeffs[0] * middle
    for k in range(1, 7):
        lap = lap + coeffs[k] * (
            extended[:, 6 + k : 6 + k + width] + extended[:, 6 - k : 6 - k + width]
        )
    for k in range(1, 7):
        lap = lap + coeffs[k] * (jnp.roll(middle, -k, axis=3) + jnp.roll(middle, k, axis=3))
    depth = middle.shape[2]
    planes_out = []
    for j in range(depth):
        plane = lap[:, :, j]
        for k in range(1, 7):
            if j + k < depth:
                plane = plane + coeffs[k] * middle[:, :, j + k]
            if j - k >= 0:
                plane = plane + coeffs[k] * middle[:, :, j - k]
        planes_out.append(plane)
    lap = jnp.stack(planes_out, axis=2)
    return -2.0 * lap + pot[None] * middle


def plane_rim(field):
    return extended_2(field, (("dom", 1),), 6)


def per_device(psi, potential, rotation):
    planes = psi.shape[1]
    first = (apply_ham(plane_rim(psi), potential, planes) - center_shift * psi) / half_width
    second = (
        2.0 / half_width * (apply_ham(plane_rim(first), potential, planes) - center_shift * first)
        - psi
    )
    filtered = second.astype(jnp.bfloat16)
    own_states = psi.shape[0]
    my_columns = lax.dynamic_slice_in_dim(
        rotation, lax.axis_index("band") * own_states, own_states, 1
    )
    piece = lax.all_gather(filtered, "band", axis=0, tiled=True)
    count = piece.shape[0]
    result = lax.dot_general(
        my_columns,
        piece.reshape(count, -1),
        (((0,), (0,)), ((), ())),
        preferred_element_type=jnp.float32,
    ).astype(jnp.bfloat16)
    return result.reshape(psi.shape)


def solution(mesh):
    in_specs = (P("band", "dom", None, None), P("dom", None, None), P())
    out_specs = P("band", "dom", None, None)
    return jax.shard_map(
        per_device, mesh=mesh, in_specs=in_specs, out_specs=out_specs, check_vma=False
    )
```

profile of v0, /device:TPU:99, one launch (start us, length us, event | category | flops | bytes accessed | tf_op | source)
XLA Modules:
  0.0 579.2 jit_solution(7823604162279824461)
XLA Ops:
  6.5 1.8 fusion.79
  8.4 3.8 collective-permute-start.1
  12.1 1.9 collective-permute-start
  14.1 1.6 fusion.80
  15.7 1.6 fusion.82
  17.3 1.6 fusion.84
  18.9 1.6 fusion.87
  20.5 1.6 fusion.89
  22.1 0.5 fusion.81
  23.2 0.5 fusion.85
  23.7 0.5 fusion.86
  25.6 13.2 %fusion.91 = (f32[32,12,2,380]{3,2,1,0:T(2,128)S(1)}, f32[32,12,2,380]{3,2,1,0:T(2,128)S(1)}) fusion(f32[32,12,2,384]{3,2,1,0:T(2,128)S(1)} %copy-done.1), kind=kLoop, calls=%fused_computation.143 | loop fusion | bytes 4669440 | tf_op jit(solution)/shard_map/jit(_roll_static)/slice | solution.py:43
  39.0 0.7 constant_dynamic-update-slice_fusion.1
  40.0 17.1 %fusion.41 = f32[32,12,2,384]{3,2,1,0:T(2,128)S(1)} fusion(f32[32,12,2,4]{3,2,1,0:T(2,128)S(1)} %get-tuple-element.62, f32[32,12,2,380]{3,2,1,0:T(2,128)S(1)} %get-tuple-element.64, f32[32,12,2,380]{3,2,1,0:T(2,128)S(1)} %get-tuple-element.63, f32[32,12,2,4]{3,2,1,0:T(2,128)S(1)} %get-tuple-element.61, f32[32,12,2,5]{3,2,1,0:T(2,128)S(1)} %get-tuple-element.58, ...), kind=kLoop, calls=%fused_computation.74 | loop fusion | flops 14450688 | bytes 30670848 | tf_op jit(solution)/shard_map/add | solution.py:43
  57.1 1.7 slice_add_fusion.7
  58.8 2.0 broadcast_multiply_fusion
  60.8 1.6 fusion.67
  62.4 1.6 fusion.69
  64.0 1.6 fusion.72
  65.6 1.6 fusion.74
  67.2 1.6 fusion.76
  71.3 6.1 %collective-permute-start.2 = (f32[32,6,2,384]{3,2,1,0:T(2,128)S(1)}, f32[32,6,2,384]{3,2,1,0:T(2,128)S(1)}, u32[]{:S(2)}, u32[]{:S(2)}) collective-permute-start(f32[32,6,2,384]{3,2,1,0:T(2,128)S(1)} %get-tuple-element.11), channel_id=1, source_target_pairs={{32,0},{64,32},{96,64},{128,96},{160,128},{192,160},{224,192},{256... | collective-permute-start | bytes 1769480 | tf_op jit(solution)/shard_map/ppermute | solution.py:28
  77.4 2.1 collective-permute-start.3
  80.6 1.6 fusion.78
  82.5 3.6 collective-permute-done.3
  86.1 18.5 %fusion.52 = f32[32,12,2,384]{3,2,1,0:T(2,128)S(1)} fusion(f32[32,12,2,3]{3,2,1,0:T(2,128)S(1)} %get-tuple-element.34, f32[32,12,2,381]{3,2,1,0:T(2,128)S(1)} %get-tuple-element.36, f32[32,12,2,381]{3,2,1,0:T(2,128)S(1)} %get-tuple-element.35, f32[32,12,2,3]{3,2,1,0:T(2,128)S(1)} %get-tuple-element.33, f32[32,12,2,4]{3,2,1,0:T(2,128)S(1)} %get-tuple-element.30, ...), kind=kLoop, calls=%fused_computation.91 | loop fusion | flops 17989632 | bytes 18874368 | tf_op jit(solution)/shard_map/add | solution.py:43
  104.6 1.7 fusion.62
  106.3 2.9 fusion.60
  109.2 422.1 %all-gather.2.cloned.1.call-done = bf16[1024,12,2,384]{3,2,1,0:T(2,128)(2,1)} async-done(((bf16[32,12,2,384]{3,2,1,0:T(2,128)(2,1)}), bf16[1024,12,2,384]{3,2,1,0:T(2,128)(2,1)}) %all-gather.2.cloned.1.call-update) | async-done | bytes 18874384 | tf_op jit(solution)/shard_map/all_gather | solution.py:74
  531.3 29.6 %reshape.7 = bf16[1024,9216]{1,0:T(8,128)(2,1)} reshape(bf16[1024,12,2,384]{3,2,1,0:T(2,128)(2,1)} %all-gather.2.cloned.1.call-done) | data formatting | bytes 37748736 | tf_op jit(solution)/shard_map/reshape | solution.py:78
  560.9 9.8 %convolution_convert_fusion = bf16[32,9216]{1,0:T(8,128)(2,1)S(1)} fusion(bf16[1024,9216]{1,0:T(8,128)(2,1)} %reshape.7, bf16[1024,1024]{1,0:T(8,128)(2,1)S(1)} %copy-done, s32[]{:T(128)S(6)} %select_n.3), kind=kOutput, calls=%fused_computation | convolution fusion | flops 604274688 | bytes 19726340 | tf_op jit(solution)/shard_map/dot_general | solution.py:76
  570.7 1.3 reshape.8
  (24 shorter events, 6.2 us)
Async XLA Ops:
  6.5 554.4 %copy-start = (bf16[1024,1024]{1,0:T(8,128)(2,1)S(1)}, bf16[1024,1024]{1,0:T(8,128)(2,1)}, u32[]{:S(2)}) copy-start(bf16[1024,1024]{1,0:T(8,128)(2,1)} %param.5) | copy-start | bytes 6291460
  6.5 7.5 %copy-start.1 = (f32[32,12,2,384]{3,2,1,0:T(2,128)S(1)}, f32[32,12,2,384]{3,2,1,0:T(2,128)}, u32[]{:S(2)}) copy-start(f32[32,12,2,384]{3,2,1,0:T(2,128)} %param.3) | copy-start | bytes 3538948
  6.5 524.7 %all-gather.2.cloned.1.call-start = ((), (), s32[]{:S(2)}) async-start(), calls=%async_computation | async-start | bytes 19464192 | tf_op jit(solution)/shard_map/all_gather | solution.py:74
  8.4 30.4 %collective-permute-start.1 = (f32[32,6,2,384]{3,2,1,0:T(2,128)S(1)}, f32[32,6,2,384]{3,2,1,0:T(2,128)S(1)}, u32[]{:S(2)}, u32[]{:S(2)}) collective-permute-start(f32[32,6,2,384]{3,2,1,0:T(2,128)S(1)} %get-tuple-element.38), channel_id=1, source_target_pairs={{0,32},{32,64},{64,96},{96,128},{128,160},{160,192},{192,224},{224... | collective-permute-start | bytes 1769480 | tf_op jit(solution)/shard_map/ppermute | solution.py:26
  12.1 27.6 %collective-permute-start = (f32[32,6,2,384]{3,2,1,0:T(2,128)S(1)}, f32[32,6,2,384]{3,2,1,0:T(2,128)S(1)}, u32[]{:S(2)}, u32[]{:S(2)}) collective-permute-start(f32[32,6,2,384]{3,2,1,0:T(2,128)S(1)} %get-tuple-element.37), channel_id=1, source_target_pairs={{32,0},{64,32},{96,64},{128,96},{160,128},{192,160},{224,192},{256... | collective-permute-start | bytes 1769480 | tf_op jit(solution)/shard_map/ppermute | solution.py:28
  24.2 0.8 copy-start.2
  71.3 11.2 %collective-permute-start.2 = (f32[32,6,2,384]{3,2,1,0:T(2,128)S(1)}, f32[32,6,2,384]{3,2,1,0:T(2,128)S(1)}, u32[]{:S(2)}, u32[]{:S(2)}) collective-permute-start(f32[32,6,2,384]{3,2,1,0:T(2,128)S(1)} %get-tuple-element.11), channel_id=1, source_target_pairs={{32,0},{64,32},{96,64},{128,96},{160,128},{192,160},{224,192},{256... | collective-permute-start | bytes 1769480 | tf_op jit(solution)/shard_map/ppermute | solution.py:28
  77.4 8.7 %collective-permute-start.3 = (f32[32,6,2,384]{3,2,1,0:T(2,128)S(1)}, f32[32,6,2,384]{3,2,1,0:T(2,128)S(1)}, u32[]{:S(2)}, u32[]{:S(2)}) collective-permute-start(f32[32,6,2,384]{3,2,1,0:T(2,128)S(1)} %get-tuple-element.12), channel_id=1, source_target_pairs={{0,32},{32,64},{64,96},{96,128},{128,160},{160,192},{192,224},{224... | collective-permute-start | bytes 1769480 | tf_op jit(solution)/shard_map/ppermute | solution.py:26
Sparse Core Ops, SparseCore 0:
  109.3 421.9 all-gather.1
where the time goes:
time: 589 us; the launch traced here: 579 us
  waiting for transfers between devices  426 us (72%)
  local copies, waits for them, and re-layouts  71.6 us (12%)
  other arithmetic  43.8 us (7%)
  between operations  14.1 us (2%)
  starting transfers between devices  13.9 us (2%)
  matrix products  9.84 us (2%)
    all_gather x1, waiting for transfers between devices, per_device(): piece = lax.all_gather(filtered, 'band', axis=0, tiled=True)  422 us
    add x2, other arithmetic, apply_ham(): lap + coeffs[k] * (jnp.roll(middle, -k, axis=3) + jnp.roll(middle, k, axi...  35.5 us
    reshape x1, local copies, waits for them, and re-layouts, per_device(): piece.reshape(count, -1)  29.6 us
    slice x14, local copies, waits for them, and re-layouts, apply_ham(): jnp.roll(middle, k, axis=3)  26.4 us
  transfers between devices with their start and end apart: 5, of which 3 were waited for; matrix products, arithmetic and copies ran while one was open for 5% of the time, Pallas kernels for 0%

commit v1 on v0

--- a/solution.py
+++ b/solution.py
@@ -71,7 +71,9 @@
     my_columns = lax.dynamic_slice_in_dim(
         rotation, lax.axis_index("band") * own_states, own_states, 1
     )
-    piece = lax.all_gather(filtered, "band", axis=0, tiled=True)
+    piece = jnp.concatenate(
+        lax.all_to_all(jnp.stack([filtered] * lax.axis_size("band")), "band", 0, 0), axis=0
+    )
     count = piece.shape[0]
     result = lax.dot_general(
         my_columns,

time: 589 us -> 1020 us (1.73)
  the two profiles are of different devices: /device:TPU:99 before, /device:TPU:189 now
where the time goes in v1:
time: 1020 us; the launch traced here: 1010 us
  waiting for transfers between devices  838 us (82%)
  local copies, waits for them, and re-layouts  90.1 us (9%)
  other arithmetic  43.1 us (4%)
  starting transfers between devices  28.2 us (3%)
    all_to_all x1, waiting for transfers between devices, per_device(): lax.all_to_all(jnp.stack([filtered] * lax.axis_size('band')), 'band', 0, 0)  834 us
    add x2, other arithmetic, apply_ham(): lap + coeffs[k] * (jnp.roll(middle, -k, axis=3) + jnp.roll(middle, k, axi...  35.5 us
    another operation x1, local copies, waits for them, and re-layouts, per_device(): piece.reshape(count, -1)  29.6 us
    slice x14, local copies, waits for them, and re-layouts, apply_ham(): jnp.roll(middle, k, axis=3)  26.4 us
  transfers between devices with their start and end apart: 5, of which 3 were waited for; matrix products, arithmetic and copies ran while one was open for 3% of the time, Pallas kernels for 0%

profile of v1, /device:TPU:189, one launch (start us, length us, event | category | flops | bytes accessed | tf_op | source)
XLA Modules:
  0.0 1010.1 jit_solution(10941734163354964685)
XLA Ops:
  0.0 1.8 fusion.79
  1.8 2.4 collective-permute-start.1
  4.2 2.1 collective-permute-start
  6.3 1.6 fusion.80
  8.0 1.6 fusion.82
  9.6 1.6 fusion.84
  11.2 1.6 fusion.87
  12.8 1.6 fusion.89
  17.8 13.2 %fusion.91 = (f32[32,12,2,380]{3,2,1,0:T(2,128)S(1)}, f32[32,12,2,380]{3,2,1,0:T(2,128)S(1)}) fusion(f32[32,12,2,384]{3,2,1,0:T(2,128)S(1)} %copy-done.1), kind=kLoop, calls=%fused_computation.143 | loop fusion | bytes 4669440 | tf_op jit(solution)/shard_map/jit(_roll_static)/slice | solution.py:43
  31.2 0.7 constant_dynamic-update-slice_fusion.1
  32.3 17.1 %fusion.41 = f32[32,12,2,384]{3,2,1,0:T(2,128)S(1)} fusion(f32[32,12,2,4]{3,2,1,0:T(2,128)S(1)} %get-tuple-element.62, f32[32,12,2,380]{3,2,1,0:T(2,128)S(1)} %get-tuple-element.64, f32[32,12,2,380]{3,2,1,0:T(2,128)S(1)} %get-tuple-element.63, f32[32,12,2,4]{3,2,1,0:T(2,128)S(1)} %get-tuple-element.61, f32[32,12,2,5]{3,2,1,0:T(2,128)S(1)} %get-tuple-element.58, ...), kind=kLoop, calls=%fused_computation.74 | loop fusion | flops 14450688 | bytes 30670848 | tf_op jit(solution)/shard_map/add | solution.py:43
  49.4 1.7 slice_add_fusion.7
  51.0 2.0 broadcast_multiply_fusion
  53.0 1.6 fusion.67
  54.6 1.6 fusion.69
  56.3 1.6 fusion.72
  57.9 1.6 fusion.74
  59.5 1.6 fusion.76
  63.6 3.6 collective-permute-start.2
  67.3 5.7 collective-permute-start.3
  74.0 1.6 fusion.78
  75.7 2.8 collective-permute-done.2
  78.4 1.2 collective-permute-done.3
  79.6 18.5 %fusion.52 = f32[32,12,2,384]{3,2,1,0:T(2,128)S(1)} fusion(f32[32,12,2,3]{3,2,1,0:T(2,128)S(1)} %get-tuple-element.34, f32[32,12,2,381]{3,2,1,0:T(2,128)S(1)} %get-tuple-element.36, f32[32,12,2,381]{3,2,1,0:T(2,128)S(1)} %get-tuple-element.35, f32[32,12,2,3]{3,2,1,0:T(2,128)S(1)} %get-tuple-element.33, f32[32,12,2,4]{3,2,1,0:T(2,128)S(1)} %get-tuple-element.30, ...), kind=kLoop, calls=%fused_computation.91 | loop fusion | flops 17989632 | bytes 18874368 | tf_op jit(solution)/shard_map/add | solution.py:43
  98.1 1.7 fusion.62
  99.8 2.2 fusion.60
  102.0 18.6 %stack.8 = bf16[32,32,12,2,384]{4,3,2,1,0:T(2,128)(2,1)} broadcast(bf16[32,12,2,384]{3,2,1,0:T(2,128)(2,1)S(1)} %fusion.60), dimensions={1,2,3,4} | broadcast | bytes 19464192 | tf_op jit(solution)/shard_map/stack | solution.py:75
  120.5 14.3 %all-to-all-start = ((bf16[32,32,12,2,384]{4,3,2,1,0:T(2,128)(2,1)}), bf16[32,32,12,2,384]{4,3,2,1,0:T(2,128)(2,1)}, u32[]{:S(2)}, u32[]{:S(2)}) async-start(bf16[32,32,12,2,384]{4,3,2,1,0:T(2,128)(2,1)} %stack.8), calls=%async_computation | async-start | bytes 37748736 | tf_op jit(solution)/shard_map/all_to_all | solution.py:75
  134.9 834.1 %all-to-all-done = bf16[32,32,12,2,384]{4,3,2,1,0:T(2,128)(2,1)} async-done(((bf16[32,32,12,2,384]{4,3,2,1,0:T(2,128)(2,1)}), bf16[32,32,12,2,384]{4,3,2,1,0:T(2,128)(2,1)}, u32[]{:S(2)}, u32[]{:S(2)}) %all-to-all-start) | async-done | bytes 18874400 | tf_op jit(solution)/shard_map/all_to_all | solution.py:75
  969.0 29.6 %reshape_reshape.3 = bf16[1024,9216]{1,0:T(8,128)(2,1)} reshape(bf16[32,32,12,2,384]{4,3,2,1,0:T(2,128)(2,1)} %all-to-all-done) | data formatting | bytes 37748736 | tf_op jit(solution)/shard_map/reshape;reshape | solution.py:80
  998.6 9.8 convolution_convert_fusion
  1008.4 1.3 reshape.6
  (24 shorter events, 7.4 us)
Async XLA Ops:
  0.0 998.6 %copy-start = (bf16[1024,1024]{1,0:T(8,128)(2,1)S(1)}, bf16[1024,1024]{1,0:T(8,128)(2,1)}, u32[]{:S(2)}) copy-start(bf16[1024,1024]{1,0:T(8,128)(2,1)} %param.5) | copy-start | bytes 6291460
  0.0 6.3 copy-start.1
  1.8 29.2 %collective-permute-start.1 = (f32[32,6,2,384]{3,2,1,0:T(2,128)S(1)}, f32[32,6,2,384]{3,2,1,0:T(2,128)S(1)}, u32[]{:S(2)}, u32[]{:S(2)}) collective-permute-start(f32[32,6,2,384]{3,2,1,0:T(2,128)S(1)} %get-tuple-element.38), channel_id=1, source_target_pairs={{0,32},{32,64},{64,96},{96,128},{128,160},{160,192},{192,224},{224... | collective-permute-start | bytes 1769480 | tf_op jit(solution)/shard_map/ppermute | solution.py:26
  4.2 27.8 %collective-permute-start = (f32[32,6,2,384]{3,2,1,0:T(2,128)S(1)}, f32[32,6,2,384]{3,2,1,0:T(2,128)S(1)}, u32[]{:S(2)}, u32[]{:S(2)}) collective-permute-start(f32[32,6,2,384]{3,2,1,0:T(2,128)S(1)} %get-tuple-element.37), channel_id=1, source_target_pairs={{32,0},{64,32},{96,64},{128,96},{160,128},{192,160},{224,192},{256... | collective-permute-start | bytes 1769480 | tf_op jit(solution)/shard_map/ppermute | solution.py:28
  16.5 0.8 copy-start.2
  63.6 14.8 %collective-permute-start.2 = (f32[32,6,2,384]{3,2,1,0:T(2,128)S(1)}, f32[32,6,2,384]{3,2,1,0:T(2,128)S(1)}, u32[]{:S(2)}, u32[]{:S(2)}) collective-permute-start(f32[32,6,2,384]{3,2,1,0:T(2,128)S(1)} %get-tuple-element.11), channel_id=1, source_target_pairs={{32,0},{64,32},{96,64},{128,96},{160,128},{192,160},{224,192},{256... | collective-permute-start | bytes 1769480 | tf_op jit(solution)/shard_map/ppermute | solution.py:28
  67.3 12.3 %collective-permute-start.3 = (f32[32,6,2,384]{3,2,1,0:T(2,128)S(1)}, f32[32,6,2,384]{3,2,1,0:T(2,128)S(1)}, u32[]{:S(2)}, u32[]{:S(2)}) collective-permute-start(f32[32,6,2,384]{3,2,1,0:T(2,128)S(1)} %get-tuple-element.12), channel_id=1, source_target_pairs={{0,32},{32,64},{64,96},{96,128},{128,160},{160,192},{192,224},{224... | collective-permute-start | bytes 1769480 | tf_op jit(solution)/shard_map/ppermute | solution.py:26
  120.5 848.5 %all-to-all-start = ((bf16[32,32,12,2,384]{4,3,2,1,0:T(2,128)(2,1)}), bf16[32,32,12,2,384]{4,3,2,1,0:T(2,128)(2,1)}, u32[]{:S(2)}, u32[]{:S(2)}) async-start(bf16[32,32,12,2,384]{4,3,2,1,0:T(2,128)(2,1)} %stack.8), calls=%async_computation | async-start | bytes 37748736 | tf_op jit(solution)/shard_map/all_to_all | solution.py:75
